TPU v7x, 256 devices: a whole 4x4x8 slice. The times are simulated.
256 devices in a mesh: gx: 16 (over z, core), gy: 16 (over y, x).
Axes of the slice: x: 4, y: 4, z: 8, core: 2. Of those that a mesh axis runs over, the one named last changes fastest.
Arguments:
- right_side: float32 [256, 128, 1024], P('gx', 'gy'), may hold values from -340 to 340
- start_guess: float32 [256, 128, 1024], P('gx', 'gy'), may hold values from -1.8 to 1.8
- couple_x: float32 [256, 128, 64], P('gx', 'gy'), may hold values from 0.3 to 3
- couple_y: float32 [256, 128, 64], P('gx', 'gy'), may hold values from 0.3 to 3
- couple_z: float32 [256, 128, 64], P('gx', 'gy'), may hold values from 0.3 to 3
- reaction: float32 [256, 128, 64], P('gx', 'gy'), may hold values from 0.01 to 0.1
Outputs:
- solution: float32 [256, 128, 1024], P('gx', 'gy')
- residual: float32 [256, 128, 1024], P('gx', 'gy')
All inputs are finite; a program needn't handle non-finite values.
Results may differ from a plain program's by a relative error of at most 0.0003.
Values sent between devices are 32-bit elements; how exact they have to be, the bound alone decides.
No kernel may reach another device: no remote copies, remote signals or barrier semaphores. Data moves between devices by JAX's collectives and lax.ppermute only.
A program may use at most 64 MiB of HBM per device.

v0:
```python
import jax
import jax.numpy as jnp
from jax import lax
from jax.sharding import PartitionSpec as P

ITERS = 2
SWEEPS = 4
FACT_SWEEPS = 3
HIGH = lax.Precision.HIGHEST


def passed_along(block, axis, distance):
    devices = range(lax.axis_size(axis))
    route = [(i - distance, i) for i in devices if i - distance in devices]
    return lax.ppermute(block, axis, route)


def padded_2(block, sides, width):
    for axis, dim in sides:
        count = lax.axis_size(axis)
        forward = [(i, i + 1) for i in range(count - 1)]
        backward = [(target, source) for source, target in forward]
        low = lax.ppermute(
            lax.slice_in_dim(block, block.shape[dim] - width, None, axis=dim), axis, forward
        )
        high = lax.ppermute(lax.slice_in_dim(block, 0, width, axis=dim), axis, backward)
        block = jnp.concatenate([low, block, high], axis=dim)
    return block


def low_shift(values, along):
    count = values.shape[along]
    blank = jnp.zeros_like(lax.slice_in_dim(values, 0, 1, axis=along))
    return jnp.concatenate([blank, lax.slice_in_dim(values, 0, count - 1, axis=along)], axis=along)


def up_shift(values, along):
    count = values.shape[along]
    blank = jnp.zeros_like(lax.slice_in_dim(values, 0, 1, axis=along))
    return jnp.concatenate([lax.slice_in_dim(values, 1, count, axis=along), blank], axis=along)


def block_gram(former, latter, count_rhs):
    cells = former.shape[0] * former.shape[1]
    left = former.reshape(cells, count_rhs, -1)
    right = latter.reshape(cells, count_rhs, -1)
    return jnp.einsum("psz,ptz->st", left, right, precision=HIGH)


def mix_block(values, matrix):
    rows_x, rows_y, flat_len = values.shape
    count_rhs = matrix.shape[0]
    split = values.reshape(rows_x * rows_y, count_rhs, flat_len // count_rhs)
    return jnp.einsum("psz,st->ptz", split, matrix, precision=HIGH).reshape(
        rows_x, rows_y, flat_len
    )


def chol_factor(gram_mat):
    low_factor = jnp.linalg.cholesky(gram_mat)
    eye_mat = jnp.eye(gram_mat.shape[0], dtype=gram_mat.dtype)
    inverse = lax.linalg.triangular_solve(low_factor, eye_mat, left_side=True, lower=True)
    return (low_factor.T, inverse.T)


def solve_small(columns, first_factor):
    hessen = jnp.concatenate(columns, axis=1)
    count_rhs = first_factor.shape[0]
    target = jnp.dot(hessen[:count_rhs].T, first_factor, precision=HIGH)
    normal = jnp.dot(hessen.T, hessen, precision=HIGH)
    low_factor = jnp.linalg.cholesky(normal)
    partial_sol = lax.linalg.triangular_solve(low_factor, target, left_side=True, lower=True)
    return lax.linalg.triangular_solve(
        low_factor, partial_sol, left_side=True, lower=True, transpose_a=True
    )


def body(right_side, start_guess, couple_x, couple_y, couple_z, reaction):
    rows_x, rows_y, flat_len = right_side.shape
    layers = couple_z.shape[2]
    count_rhs = flat_len // layers
    depth = jnp.arange(flat_len, dtype=jnp.int32) % layers
    keep_first = (depth != 0).astype(jnp.float32)
    keep_last = (depth != layers - 1).astype(jnp.float32)

    def low_z(values):
        return low_shift(values, 2) * keep_first

    def up_z(values):
        return up_shift(values, 2) * keep_last

    def tiled(values):
        return jnp.tile(values, (1, 1, count_rhs))

    edge_x = passed_along(couple_x[-1:], "gx", 1)
    edge_y = passed_along(couple_y[:, -1:], "gy", 1)
    after_x = tiled(couple_x)
    after_y = tiled(couple_y)
    after_z = tiled(couple_z)
    before_x = tiled(jnp.concatenate([edge_x, couple_x[:-1]], axis=0))
    before_y = tiled(jnp.concatenate([edge_y, couple_y[:, :-1]], axis=1))
    before_z = low_z(after_z)
    diagonal = tiled(reaction) + after_x + before_x + after_y + before_y + after_z + before_z

    def apply_op(values):
        padded = padded_2(values, (("gx", 0), ("gy", 1)), 1)
        centre = padded[1:-1, 1:-1]
        return (
            diagonal * centre
            - after_x * padded[2:, 1:-1]
            - before_x * padded[:-2, 1:-1]
            - after_y * padded[1:-1, 2:]
            - before_y * padded[1:-1, :-2]
            - after_z * up_z(centre)
            - before_z * low_z(centre)
        )

    lows = (low_shift(after_x, 0), low_shift(after_y, 1), before_z)
    ups = (
        up_shift(jnp.ones_like(after_x), 0) * after_x,
        up_shift(jnp.ones_like(after_y), 1) * after_y,
        after_z,
    )
    pivots = diagonal
    for repeat in range(FACT_SWEEPS):
        inv_now = 1.0 / pivots
        pivots = (
            diagonal
            - lows[0] * lows[0] * low_shift(inv_now, 0)
            - lows[1] * lows[1] * low_shift(inv_now, 1)
            - lows[2] * lows[2] * low_z(inv_now)
        )
    inv_piv = 1.0 / pivots

    def total_gram(former, latter):
        return lax.psum(block_gram(former, latter, count_rhs), ("gx", "gy"))

    start_res = right_side - apply_op(start_guess)
    first_factor, first_inv = chol_factor(total_gram(start_res, start_res))
    basis_set = [mix_block(start_res, first_inv)]
    precond_set = []
    image_set = []
    columns = []
    for column in range(ITERS):
        source = basis_set[column]
        lower_sol = inv_piv * source
        for precondition_repeat in range(SWEEPS):
            lower_sol = inv_piv * (
                source
                + lows[0] * low_shift(lower_sol, 0)
                + lows[1] * low_shift(lower_sol, 1)
                + lows[2] * low_z(lower_sol)
            )
        upper_sol = lower_sol
        for precondition_repeat in range(SWEEPS):
            upper_sol = lower_sol + inv_piv * (
                ups[0] * up_shift(upper_sol, 0)
                + ups[1] * up_shift(upper_sol, 1)
                + ups[2] * up_z(upper_sol)
            )
        image = apply_op(upper_sol)
        precond_set.append(upper_sol)
        image_set.append(image)
        local_proj = jnp.stack([block_gram(member, image, count_rhs) for member in basis_set])
        stacked = lax.psum(local_proj, ("gx", "gy"))
        projections = [stacked[member] for member in range(len(basis_set))]
        removed = mix_block(basis_set[0], projections[0])
        for member in range(1, len(basis_set)):
            removed = removed + mix_block(basis_set[member], projections[member])
        perp = image - removed
        next_factor, next_inv = chol_factor(total_gram(perp, perp))
        if column + 1 < ITERS:
            basis_set.append(mix_block(perp, next_inv))
        blank = jnp.zeros(((ITERS - 1 - column) * count_rhs, count_rhs), dtype=next_factor.dtype)
        columns.append(jnp.concatenate(projections + [next_factor, blank], axis=0))
    coeffs = solve_small(columns, first_factor)
    solution = start_guess
    for column in range(ITERS):
        solution = solution + mix_block(
            precond_set[column], coeffs[column * count_rhs : (column + 1) * count_rhs]
        )
    residual = right_side - apply_op(solution)
    return (solution, residual)


def solution(mesh):
    return jax.shard_map(
        body,
        mesh=mesh,
        in_specs=(
            P("gx", "gy", None),
            P("gx", "gy", None),
            P("gx", "gy", None),
            P("gx", "gy", None),
            P("gx", "gy", None),
            P("gx", "gy", None),
        ),
        out_specs=(P("gx", "gy", None), P("gx", "gy", None)),
        check_vma=False,
    )
```

profile of v0, /device:TPU:40, one launch (start us, length us, event | category | flops | bytes accessed | tf_op | source)
XLA Modules:
  0.0 608.5 jit_solution(9430777300080090725)
XLA Ops:
  3.4 3.6 collective-permute-start.2
  9.3 3.4 collective-permute-start.1
  12.7 2.3 fusion.87
  20.4 2.3 tile.29
  26.3 2.4 tile.63
  29.7 4.6 collective-permute-start.4
  37.3 2.3 tile.67
  39.6 3.6 collective-permute-done.5
  43.2 3.8 fusion.36
  49.3 3.1 convolution_bitcast_fusion.12
  52.4 2.5 copy.35
  57.6 77.3 %psum.35 = f32[16,16]{0,1:T(8,128)S(1)} all-reduce(f32[16,16]{0,1:T(8,128)S(1)} %convolution_bitcast_fusion.12), channel_id=1, replica_groups=mesh['gx'=16,'gy'=16] {'gx','gy'}, use_global_device_ids=true, to_apply=%region_0.1 | all-reduce | flops 256 | bytes 2048 | tf_op jit(solution)/shard_map/psum | solution.py:136
  142.2 2.3 reshape.113
  153.0 2.8 collective-permute-start.6
  157.7 3.3 collective-permute-done.7
  161.1 4.6 collective-permute-start.8
  168.1 6.2 %collective-permute-done.9 = f32[18,1,1024]{2,1,0:T(1,128)S(1)} collective-permute-done((f32[18,1,1024]{2,1,0:T(1,128)S(1)}, f32[18,1,1024]{2,1,0:T(1,128)S(1)}, u32[]{:S(2)}, u32[]{:S(2)}) %collective-permute-start.9) | collective-permute-done | bytes 73760 | tf_op jit(solution)/shard_map/ppermute | solution.py:23
  178.0 2.5 copy.37
  182.5 71.4 %psum.36 = f32[16,16]{0,1:T(8,128)S(1)} all-reduce(f32[16,16]{0,1:T(8,128)S(1)} %convolution_bitcast_fusion.10), channel_id=1, replica_groups=mesh['gx'=16,'gy'=16] {'gx','gy'}, use_global_device_ids=true, to_apply=%region_3.6 | all-reduce | flops 256 | bytes 2048 | tf_op jit(solution)/shard_map/psum | solution.py:165
  253.9 2.4 convolution_bitcast_fusion.3
  256.3 2.5 copy.39
  258.8 2.3 reshape.115
  265.4 2.5 copy.44
  268.0 3.1 convolution_bitcast_fusion.9
  271.0 74.0 %psum.37 = f32[16,16]{0,1:T(8,128)S(1)} all-reduce(f32[16,16]{0,1:T(8,128)S(1)} %convolution_bitcast_fusion.9), channel_id=1, replica_groups=mesh['gx'=16,'gy'=16] {'gx','gy'}, use_global_device_ids=true, to_apply=%region_4.7 | all-reduce | flops 256 | bytes 2048 | tf_op jit(solution)/shard_map/psum | solution.py:136
  349.4 2.4 convolution_bitcast_fusion.2
  351.8 2.5 copy.45
  354.3 2.3 reshape.117
  364.9 2.9 collective-permute-start.10
  372.3 2.6 copy.56
  375.0 4.6 collective-permute-start.12
  384.0 2.5 copy.58
  388.1 2.9 fusion.15
  393.3 2.6 copy.46
  398.7 75.0 %psum.38 = f32[2,16,16]{1,2,0:T(8,128)S(1)} all-reduce(f32[2,16,16]{1,2,0:T(8,128)S(1)} %pad_maximum_fusion.39), channel_id=1, replica_groups=mesh['gx'=16,'gy'=16] {'gx','gy'}, use_global_device_ids=true, to_apply=%region_5.8 | all-reduce | flops 512 | bytes 4096 | tf_op jit(solution)/shard_map/psum | solution.py:165
  476.7 2.4 add.472
  483.3 3.1 convolution_bitcast_fusion.5
  486.5 74.9 %psum.39 = f32[16,16]{0,1:T(8,128)S(1)} all-reduce(f32[16,16]{0,1:T(8,128)S(1)} %convolution_bitcast_fusion.5), channel_id=1, replica_groups=mesh['gx'=16,'gy'=16] {'gx','gy'}, use_global_device_ids=true, to_apply=%region_6.9 | all-reduce | flops 256 | bytes 2048 | tf_op jit(solution)/shard_map/psum | solution.py:136
  565.4 2.9 cholesky.41
  569.6 2.4 custom-call.13
  573.9 2.5 copy.57
  576.4 2.4 reshape.121
  580.2 2.5 copy.59
  582.6 2.4 reshape.123
  588.3 2.4 collective-permute-start.15
  590.7 2.8 collective-permute-done.15
  593.6 4.7 collective-permute-start.16
  600.6 6.2 %collective-permute-done.17 = f32[18,1,1024]{2,1,0:T(1,128)S(1)} collective-permute-done((f32[18,1,1024]{2,1,0:T(1,128)S(1)}, f32[18,1,1024]{2,1,0:T(1,128)S(1)}, u32[]{:S(2)}, u32[]{:S(2)}) %collective-permute-start.17) | collective-permute-done | bytes 73760 | tf_op jit(solution)/shard_map/ppermute | solution.py:23
  (224 shorter events, 103.6 us)
Async XLA Ops:
  0.6 6.4 %copy-start.24 = (f32[16,8,64]{2,1,0:T(8,128)S(1)}, f32[16,8,64]{2,1,0:T(8,128)}, u32[]{:S(2)}) copy-start(f32[16,8,64]{2,1,0:T(8,128)} %param.11) | copy-start | bytes 98308
  0.6 8.6 %copy-start.23 = (f32[16,8,64]{2,1,0:T(8,128)S(1)}, f32[16,8,64]{2,1,0:T(8,128)}, u32[]{:S(2)}) copy-start(f32[16,8,64]{2,1,0:T(8,128)} %param.12) | copy-start | bytes 98308
  1.5 27.3 %collective-permute-start.3 = (f32[1,8,1024]{2,1,0:T(8,128)S(1)}, f32[1,8,1024]{2,1,0:T(8,128)S(1)}, u32[]{:S(2)}, u32[]{:S(2)}) collective-permute-start(f32[1,8,1024]{2,1,0:T(8,128)S(1)} %get-tuple-element.31), channel_id=1, source_target_pairs={{0,16},{16,32},{32,48},{48,64},{64,80},{80,96},{96,112},{112,128},... | collective-permute-start | bytes 98312 | tf_op jit(solution)/shard_map/ppermute | solution.py:23
  3.4 25.4 %collective-permute-start.2 = (f32[1,8,1024]{2,1,0:T(8,128)S(1)}, f32[1,8,1024]{2,1,0:T(8,128)S(1)}, u32[]{:S(2)}, u32[]{:S(2)}) collective-permute-start(f32[1,8,1024]{2,1,0:T(8,128)S(1)} %get-tuple-element.30), channel_id=1, source_target_pairs={{16,0},{32,16},{48,32},{64,48},{80,64},{96,80},{112,96},{128,112},... | collective-permute-start | bytes 98312 | tf_op jit(solution)/shard_map/ppermute | solution.py:26
  7.1 18.2 %collective-permute-start = (f32[1,8,64]{2,1,0:T(8,128)S(1)}, f32[1,8,64]{2,1,0:T(8,128)S(1)}, u32[]{:S(2)}, u32[]{:S(2)}) collective-permute-start(f32[1,8,64]{2,1,0:T(8,128)S(1)} %slice.369), channel_id=1, source_target_pairs={{0,16},{16,32},{32,48},{48,64},{64,80},{80,96},{96,112},{112,128},... | collective-permute-start | bytes 6152 | tf_op jit(solution)/shard_map/ppermute | solution.py:15
  9.3 26.9 %collective-permute-start.1 = (f32[16,1,64]{2,1,0:T(1,128)S(1)}, f32[16,1,64]{2,1,0:T(1,128)S(1)}, u32[]{:S(2)}, u32[]{:S(2)}) collective-permute-start(f32[16,1,64]{2,1,0:T(1,128)S(1)} %slice.371), channel_id=1, source_target_pairs={{0,1},{1,2},{2,3},{3,4},{4,5},{5,6},{6,7},{7,8},{8,9},{9,10},{10,1... | collective-permute-start | bytes 12296 | tf_op jit(solution)/shard_map/ppermute | solution.py:15
  15.1 0.8 copy-start.25
  17.7 1.6 copy-start.26
  26.3 2.4 copy-start.7
  28.8 0.8 copy-start.22
  29.7 9.9 %collective-permute-start.4 = (f32[18,1,1024]{2,1,0:T(1,128)S(1)}, f32[18,1,1024]{2,1,0:T(1,128)S(1)}, u32[]{:S(2)}, u32[]{:S(2)}) collective-permute-start(f32[18,1,1024]{2,1,0:T(1,128)S(1)} %get-tuple-element.14), channel_id=1, source_target_pairs={{1,0},{2,1},{3,2},{4,3},{5,4},{6,5},{7,6},{8,7},{9,8},{10,9},{11,1... | collective-permute-start | bytes 221192 | tf_op jit(solution)/shard_map/ppermute | solution.py:26
  34.3 8.9 %collective-permute-start.5 = (f32[18,1,1024]{2,1,0:T(1,128)S(1)}, f32[18,1,1024]{2,1,0:T(1,128)S(1)}, u32[]{:S(2)}, u32[]{:S(2)}) collective-permute-start(f32[18,1,1024]{2,1,0:T(1,128)S(1)} %get-tuple-element.15), channel_id=1, source_target_pairs={{0,1},{1,2},{2,3},{3,4},{4,5},{5,6},{6,7},{7,8},{8,9},{9,10},{10,1... | collective-permute-start | bytes 221192 | tf_op jit(solution)/shard_map/ppermute | solution.py:23
  55.9 0.8 copy-start.16
  140.7 1.5 copy-start.3
  146.5 1.0 copy-start.5
  152.9 21.3 %copy-start = (f32[16,8,1024]{2,1,0:T(8,128)}, f32[16,8,1024]{2,1,0:T(8,128)S(1)}, u32[]{:S(2)}) copy-start(f32[16,8,1024]{2,1,0:T(8,128)S(1)} %multiply_add_fusion.4) | copy-start | bytes 1572868
  153.0 4.8 collective-permute-start.6
  155.8 5.2 collective-permute-start.7
  161.1 6.9 %collective-permute-start.8 = (f32[18,1,1024]{2,1,0:T(1,128)S(1)}, f32[18,1,1024]{2,1,0:T(1,128)S(1)}, u32[]{:S(2)}, u32[]{:S(2)}) collective-permute-start(f32[18,1,1024]{2,1,0:T(1,128)S(1)} %get-tuple-element.12), channel_id=1, source_target_pairs={{1,0},{2,1},{3,2},{4,3},{5,4},{6,5},{7,6},{8,7},{9,8},{10,9},{11,1... | collective-permute-start | bytes 221192 | tf_op jit(solution)/shard_map/ppermute | solution.py:26
  165.8 8.5 %copy-start.10 = (f32[16,8,1024]{2,1,0:T(8,128)S(1)}, f32[16,8,1024]{2,1,0:T(8,128)}, u32[]{:S(2)}) copy-start(f32[16,8,1024]{2,1,0:T(8,128)} %tile.63) | copy-start | bytes 1572868
  165.8 8.5 %copy-start.12 = (f32[16,8,1024]{2,1,0:T(8,128)S(1)}, f32[16,8,1024]{2,1,0:T(8,128)}, u32[]{:S(2)}) copy-start(f32[16,8,1024]{2,1,0:T(8,128)} %tile.67) | copy-start | bytes 1572868
  165.8 8.5 %collective-permute-start.9 = (f32[18,1,1024]{2,1,0:T(1,128)S(1)}, f32[18,1,1024]{2,1,0:T(1,128)S(1)}, u32[]{:S(2)}, u32[]{:S(2)}) collective-permute-start(f32[18,1,1024]{2,1,0:T(1,128)S(1)} %get-tuple-element.13), channel_id=1, source_target_pairs={{0,1},{1,2},{2,3},{3,4},{4,5},{5,6},{6,7},{7,8},{8,9},{9,10},{10,1... | collective-permute-start | bytes 221192 | tf_op jit(solution)/shard_map/ppermute | solution.py:23
  357.7 1.0 copy-start.6
  364.1 0.8 copy-start.1
  364.9 10.0 %collective-permute-start.10 = (f32[1,8,1024]{2,1,0:T(8,128)S(1)}, f32[1,8,1024]{2,1,0:T(8,128)S(1)}, u32[]{:S(2)}, u32[]{:S(2)}) collective-permute-start(f32[1,8,1024]{2,1,0:T(8,128)S(1)} %get-tuple-element.23), channel_id=1, source_target_pairs={{16,0},{32,16},{48,32},{64,48},{80,64},{96,80},{112,96},{128,112},... | collective-permute-start | bytes 98312 | tf_op jit(solution)/shard_map/ppermute | solution.py:26
  367.9 7.0 %collective-permute-start.11 = (f32[1,8,1024]{2,1,0:T(8,128)S(1)}, f32[1,8,1024]{2,1,0:T(8,128)S(1)}, u32[]{:S(2)}, u32[]{:S(2)}) collective-permute-start(f32[1,8,1024]{2,1,0:T(8,128)S(1)} %get-tuple-element.22), channel_id=1, source_target_pairs={{0,16},{16,32},{32,48},{48,64},{64,80},{80,96},{96,112},{112,128},... | collective-permute-start | bytes 98312 | tf_op jit(solution)/shard_map/ppermute | solution.py:23
  372.3 2.6 copy-start.2
  375.0 11.5 %collective-permute-start.12 = (f32[18,1,1024]{2,1,0:T(1,128)S(1)}, f32[18,1,1024]{2,1,0:T(1,128)S(1)}, u32[]{:S(2)}, u32[]{:S(2)}) collective-permute-start(f32[18,1,1024]{2,1,0:T(1,128)S(1)} %get-tuple-element.10), channel_id=1, source_target_pairs={{1,0},{2,1},{3,2},{4,3},{5,4},{6,5},{7,6},{8,7},{9,8},{10,9},{11,1... | collective-permute-start | bytes 221192 | tf_op jit(solution)/shard_map/ppermute | solution.py:26
  379.6 8.4 %collective-permute-start.13 = (f32[18,1,1024]{2,1,0:T(1,128)S(1)}, f32[18,1,1024]{2,1,0:T(1,128)S(1)}, u32[]{:S(2)}, u32[]{:S(2)}) collective-permute-start(f32[18,1,1024]{2,1,0:T(1,128)S(1)} %get-tuple-element.11), channel_id=1, source_target_pairs={{0,1},{1,2},{2,3},{3,4},{4,5},{5,6},{6,7},{7,8},{8,9},{9,10},{10,1... | collective-permute-start | bytes 221192 | tf_op jit(solution)/shard_map/ppermute | solution.py:23
  393.3 2.6 copy-start.4
  395.9 1.9 copy-start.14
  395.9 2.0 copy-start.18
  473.6 1.0 copy-start.15
  476.7 2.4 copy-start.17
  483.3 89.2 %copy-start.20 = (f32[128,16,64]{0,1,2:T(8,128)S(1)}, f32[128,16,64]{0,1,2:T(8,128)}, u32[]{:S(2)}) copy-start(f32[128,16,64]{0,1,2:T(8,128)} %copy.56) | copy-start | bytes 1572868
  576.4 2.4 copy-start.21
  582.6 2.4 copy-start.8
  586.3 20.5 %copy-start.9 = (f32[16,8,1024]{2,1,0:T(8,128)}, f32[16,8,1024]{2,1,0:T(8,128)S(1)}, u32[]{:S(2)}) copy-start(f32[16,8,1024]{2,1,0:T(8,128)S(1)} %add_add_fusion) | copy-start | bytes 1572868
  586.3 4.3 collective-permute-start.14
  588.3 5.2 collective-permute-start.15
  593.6 7.0 %collective-permute-start.16 = (f32[18,1,1024]{2,1,0:T(1,128)S(1)}, f32[18,1,1024]{2,1,0:T(1,128)S(1)}, u32[]{:S(2)}, u32[]{:S(2)}) collective-permute-start(f32[18,1,1024]{2,1,0:T(1,128)S(1)} %get-tuple-element.8), channel_id=1, source_target_pairs={{1,0},{2,1},{3,2},{4,3},{5,4},{6,5},{7,6},{8,7},{9,8},{10,9},{11,1... | collective-permute-start | bytes 221192 | tf_op jit(solution)/shard_map/ppermute | solution.py:26
  598.2 8.5 %copy-start.11 = (f32[16,8,1024]{2,1,0:T(8,128)S(1)}, f32[16,8,1024]{2,1,0:T(8,128)}, u32[]{:S(2)}) copy-start(f32[16,8,1024]{2,1,0:T(8,128)} %tile.63) | copy-start | bytes 1572868
  598.3 8.5 %copy-start.13 = (f32[16,8,1024]{2,1,0:T(8,128)S(1)}, f32[16,8,1024]{2,1,0:T(8,128)}, u32[]{:S(2)}) copy-start(f32[16,8,1024]{2,1,0:T(8,128)} %tile.67) | copy-start | bytes 1572868
  598.3 8.5 %copy-start.19 = (f32[16,8,1024]{2,1,0:T(8,128)S(1)}, f32[16,8,1024]{2,1,0:T(8,128)}, u32[]{:S(2)}) copy-start(f32[16,8,1024]{2,1,0:T(8,128)} %param.9) | copy-start | bytes 1572868
  598.3 8.5 %collective-permute-start.17 = (f32[18,1,1024]{2,1,0:T(1,128)S(1)}, f32[18,1,1024]{2,1,0:T(1,128)S(1)}, u32[]{:S(2)}, u32[]{:S(2)}) collective-permute-start(f32[18,1,1024]{2,1,0:T(1,128)S(1)} %get-tuple-element.9), channel_id=1, source_target_pairs={{0,1},{1,2},{2,3},{3,4},{4,5},{5,6},{6,7},{7,8},{8,9},{9,10},{10,1... | collective-permute-start | bytes 221192 | tf_op jit(solution)/shard_map/ppermute | solution.py:23
where the time goes:
time: 617 us; the launch traced here: 609 us
  blocking collectives  373 us (60%)
  local copies, waits for them, and re-layouts  87.7 us (14%)
  starting transfers between devices  51.7 us (8%)
  other arithmetic  44.9 us (7%)
  matrix products  26 us (4%)
  waiting for transfers between devices  23.7 us (4%)
    psum x3, blocking collectives, total_gram(): return lax.psum(block_gram(former, latter, count_rhs), ('gx', 'gy'))  226 us
    psum x2, blocking collectives, body(): stacked = lax.psum(local_proj, ('gx', 'gy'))  146 us
    ppermute x8, starting transfers between devices, padded_2(): lax.ppermute(lax.slice_in_dim(block, 0, width, axis=dim), axis, backward)  29.8 us
    ppermute x8, waiting for transfers between devices, padded_2(): lax.ppermute(lax.slice_in_dim(block, block.shape[dim] - width, None, axis...  23.7 us
    ppermute x8, starting transfers between devices, padded_2(): lax.ppermute(lax.slice_in_dim(block, block.shape[dim] - width, None, axis...  16.3 us
    another operation x14, local copies, waits for them, and re-layouts, tiled(): return jnp.tile(values, (1, 1, count_rhs))  16.1 us
    dot_general x6, matrix products, block_gram(): return jnp.einsum('psz,ptz->st', left, right, precision=HIGH)  14 us
  transfers between devices with their start and end apart: 18, of which 6 were waited for; matrix products, arithmetic and copies ran while one was open for 5% of the time, Pallas kernels for 0%

commit v1 on v0

--- a/solution.py
+++ b/solution.py
@@ -162,7 +162,8 @@
         precond_set.append(upper_sol)
         image_set.append(image)
         local_proj = jnp.stack([block_gram(member, image, count_rhs) for member in basis_set])
-        stacked = lax.psum(local_proj, ("gx", "gy"))
+        reached = lax.all_gather(local_proj, axis_name=("gx", "gy"))
+        stacked = jnp.sum(reached, axis=0)
         projections = [stacked[member] for member in range(len(basis_set))]
         removed = mix_block(basis_set[0], projections[0])
         for member in range(1, len(basis_set)):

time: 617 us -> 754 us (1.22)
  blocking collectives: 373 us -> 495 us
  other arithmetic: 44.9 us -> 53.3 us
    all_gather x0 -> x2, blocking collectives: none -> 265 us  [body(): reached = lax.all_gather(local_proj, axis_name=('gx', 'gy'))]
    psum x2 -> x0, blocking collectives: 146 us -> none  [body(): stacked = lax.psum(local_proj, ('gx', 'gy'))]
  transfers between devices with their start and end apart: 18 -> 18, of which waited for: 6 -> 6; matrix products, arithmetic and copies ran while one was open for 5% -> 4% of each run, Pallas kernels for 0% -> 0%
where the time goes in v1:
time: 754 us; the launch traced here: 746 us
  blocking collectives  495 us (66%)
  local copies, waits for them, and re-layouts  87.1 us (12%)
  starting transfers between devices  54.8 us (7%)
  other arithmetic  53.3 us (7%)
  matrix products  30.4 us (4%)
  waiting for transfers between devices  24.1 us (3%)
    all_gather x2, blocking collectives, body(): reached = lax.all_gather(local_proj, axis_name=('gx', 'gy'))  265 us
    psum x3, blocking collectives, total_gram(): return lax.psum(block_gram(former, latter, count_rhs), ('gx', 'gy'))  229 us
    ppermute x8, starting transfers between devices, padded_2(): lax.ppermute(lax.slice_in_dim(block, 0, width, axis=dim), axis, backward)  33.8 us
    ppermute x8, waiting for transfers between devices, padded_2(): lax.ppermute(lax.slice_in_dim(block, block.shape[dim] - width, None, axis...  24 us
    another operation x14, local copies, waits for them, and re-layouts, tiled(): return jnp.tile(values, (1, 1, count_rhs))  16.9 us
    ppermute x8, starting transfers between devices, padded_2(): lax.ppermute(lax.slice_in_dim(block, block.shape[dim] - width, None, axis...  15.4 us
  transfers between devices with their start and end apart: 18, of which 6 were waited for; matrix products, arithmetic and copies ran while one was open for 4% of the time, Pallas kernels for 0%

profile of v1, /device:TPU:40, one launch (start us, length us, event | category | flops | bytes accessed | tf_op | source)
XLA Modules:
  0.0 745.9 jit_solution(17148361328216369678)
XLA Ops:
  3.4 3.6 collective-permute-start.2
  10.8 3.4 collective-permute-start.1
  14.2 2.3 fusion.87
  22.7 2.3 tile.29
  28.7 2.3 tile.63
  32.1 4.6 collective-permute-start.4
  42.0 3.6 collective-permute-done.5
  45.6 3.9 fusion.36
  51.8 3.1 convolution_bitcast_fusion.12
  54.9 2.5 copy.56
  60.1 77.2 %psum.21 = f32[16,16]{0,1:T(8,128)S(1)} all-reduce(f32[16,16]{0,1:T(8,128)S(1)} %convolution_bitcast_fusion.12), channel_id=1, replica_groups=mesh['gx'=16,'gy'=16] {'gx','gy'}, use_global_device_ids=true, to_apply=%region_0.1 | all-reduce | flops 256 | bytes 2048 | tf_op jit(solution)/shard_map/psum | solution.py:136
  154.7 2.8 collective-permute-start.6
  159.4 3.3 collective-permute-done.7
  162.8 4.6 collective-permute-start.8
  169.6 6.2 collective-permute-done.9
  179.6 2.5 copy.58
  184.1 122.7 %all-gather = f32[4096,16]{1,0:T(8,128)} all-gather(f32[16,16]{1,0:T(8,128)S(1)} %convolution_bitcast_fusion.10), channel_id=2, replica_groups=mesh['gx'=16,'gy'=16] {'gx','gy'}, dimensions={0}, use_global_device_ids=true | all-gather | bytes 263168 | tf_op jit(solution)/shard_map/all_gather | solution.py:165
  308.7 2.5 convolution_bitcast_fusion.3
  311.2 2.5 copy.60
  313.7 2.4 reshape.117
  320.4 2.5 copy.64
  322.9 3.1 convolution_bitcast_fusion.9
  326.0 76.0 %psum.22 = f32[16,16]{0,1:T(8,128)S(1)} all-reduce(f32[16,16]{0,1:T(8,128)S(1)} %convolution_bitcast_fusion.9), channel_id=1, replica_groups=mesh['gx'=16,'gy'=16] {'gx','gy'}, use_global_device_ids=true, to_apply=%region_4.7 | all-reduce | flops 256 | bytes 2048 | tf_op jit(solution)/shard_map/psum | solution.py:136
  406.3 2.4 convolution_bitcast_fusion.2
  408.7 2.5 copy.65
  421.8 4.8 collective-permute-start.10
  430.8 2.5 copy.74
  434.8 4.6 collective-permute-start.12
  443.9 2.5 copy.76
  447.8 2.9 fusion.15
  450.7 2.4 reshape.120
  453.1 2.5 copy.66
  459.4 142.5 %all-gather.1 = f32[512,16,16]{2,1,0:T(8,128)} all-gather(f32[2,16,16]{2,1,0:T(8,128)S(1)} %pad_maximum_fusion.39), channel_id=3, replica_groups=mesh['gx'=16,'gy'=16] {'gx','gy'}, dimensions={0}, use_global_device_ids=true | all-gather | bytes 526336 | tf_op jit(solution)/shard_map/all_gather | solution.py:165
  602.0 2.5 reduce_sum.19
  614.0 3.1 convolution_bitcast_fusion.5
  617.1 76.1 %psum.23 = f32[16,16]{0,1:T(8,128)S(1)} all-reduce(f32[16,16]{0,1:T(8,128)S(1)} %convolution_bitcast_fusion.5), channel_id=1, replica_groups=mesh['gx'=16,'gy'=16] {'gx','gy'}, use_global_device_ids=true, to_apply=%region_6.9 | all-reduce | flops 256 | bytes 2048 | tf_op jit(solution)/shard_map/psum | solution.py:136
  697.4 2.9 cholesky.41
  701.8 2.4 custom-call.13
  704.5 2.5 convolution_bitcast_fusion.1
  707.0 2.5 copy.75
  709.5 2.4 reshape.123
  711.8 2.5 convolution_bitcast_fusion
  714.3 2.5 copy.77
  720.4 4.1 collective-permute-start.14
  726.5 3.3 collective-permute-done.15
  729.9 4.6 collective-permute-start.16
  736.7 6.2 collective-permute-done.17
  742.9 2.8 fusion.5
  (211 shorter events, 113.9 us)
Async XLA Ops:
  0.6 18.4 %copy-start.16 = (f32[16,8,64]{2,1,0:T(8,128)S(1)}, f32[16,8,64]{2,1,0:T(8,128)}, u32[]{:S(2)}) copy-start(f32[16,8,64]{2,1,0:T(8,128)} %param.11) | copy-start | bytes 98308
  0.6 18.0 %copy-start.15 = (f32[16,8,64]{2,1,0:T(8,128)S(1)}, f32[16,8,64]{2,1,0:T(8,128)}, u32[]{:S(2)}) copy-start(f32[16,8,64]{2,1,0:T(8,128)} %param.12) | copy-start | bytes 98308
  1.5 29.6 %collective-permute-start.3 = (f32[1,8,1024]{2,1,0:T(8,128)S(1)}, f32[1,8,1024]{2,1,0:T(8,128)S(1)}, u32[]{:S(2)}, u32[]{:S(2)}) collective-permute-start(f32[1,8,1024]{2,1,0:T(8,128)S(1)} %get-tuple-element.31), channel_id=1, source_target_pairs={{0,16},{16,32},{32,48},{48,64},{64,80},{80,96},{96,112},{112,128},... | collective-permute-start | bytes 98312 | tf_op jit(solution)/shard_map/ppermute | solution.py:23
  3.4 27.7 %collective-permute-start.2 = (f32[1,8,1024]{2,1,0:T(8,128)S(1)}, f32[1,8,1024]{2,1,0:T(8,128)S(1)}, u32[]{:S(2)}, u32[]{:S(2)}) collective-permute-start(f32[1,8,1024]{2,1,0:T(8,128)S(1)} %get-tuple-element.30), channel_id=1, source_target_pairs={{16,0},{32,16},{48,32},{64,48},{80,64},{96,80},{112,96},{128,112},... | collective-permute-start | bytes 98312 | tf_op jit(solution)/shard_map/ppermute | solution.py:26
  7.7 19.9 %collective-permute-start = (f32[1,8,64]{2,1,0:T(8,128)S(1)}, f32[1,8,64]{2,1,0:T(8,128)S(1)}, u32[]{:S(2)}, u32[]{:S(2)}) collective-permute-start(f32[1,8,64]{2,1,0:T(8,128)S(1)} %slice.369), channel_id=1, source_target_pairs={{0,16},{16,32},{32,48},{48,64},{64,80},{80,96},{96,112},{112,128},... | collective-permute-start | bytes 6152 | tf_op jit(solution)/shard_map/ppermute | solution.py:15
  10.8 27.8 %collective-permute-start.1 = (f32[16,1,64]{2,1,0:T(1,128)S(1)}, f32[16,1,64]{2,1,0:T(1,128)S(1)}, u32[]{:S(2)}, u32[]{:S(2)}) collective-permute-start(f32[16,1,64]{2,1,0:T(1,128)S(1)} %slice.371), channel_id=1, source_target_pairs={{0,1},{1,2},{2,3},{3,4},{4,5},{5,6},{6,7},{7,8},{8,9},{9,10},{10,1... | collective-permute-start | bytes 12296 | tf_op jit(solution)/shard_map/ppermute | solution.py:15
  16.5 5.1 copy-start.17
  21.7 9.4 %copy-start.7 = (f32[16,8,1024]{2,1,0:T(8,128)S(1)}, f32[16,8,1024]{2,1,0:T(8,128)}, u32[]{:S(2)}) copy-start(f32[16,8,1024]{2,1,0:T(8,128)} %param.10) | copy-start | bytes 1572868
  31.1 0.9 copy-start.14
  32.1 9.9 %collective-permute-start.4 = (f32[18,1,1024]{2,1,0:T(1,128)S(1)}, f32[18,1,1024]{2,1,0:T(1,128)S(1)}, u32[]{:S(2)}, u32[]{:S(2)}) collective-permute-start(f32[18,1,1024]{2,1,0:T(1,128)S(1)} %get-tuple-element.14), channel_id=1, source_target_pairs={{1,0},{2,1},{3,2},{4,3},{5,4},{6,5},{7,6},{8,7},{9,8},{10,9},{11,1... | collective-permute-start | bytes 221192 | tf_op jit(solution)/shard_map/ppermute | solution.py:26
  36.6 8.9 %collective-permute-start.5 = (f32[18,1,1024]{2,1,0:T(1,128)S(1)}, f32[18,1,1024]{2,1,0:T(1,128)S(1)}, u32[]{:S(2)}, u32[]{:S(2)}) collective-permute-start(f32[18,1,1024]{2,1,0:T(1,128)S(1)} %get-tuple-element.15), channel_id=1, source_target_pairs={{0,1},{1,2},{2,3},{3,4},{4,5},{5,6},{6,7},{7,8},{8,9},{9,10},{10,1... | collective-permute-start | bytes 221192 | tf_op jit(solution)/shard_map/ppermute | solution.py:23
  58.5 0.8 copy-start.13
  143.4 3.8 copy-start.3
  147.2 2.1 copy-start.5
  154.1 21.7 %copy-start.10 = (f32[16,8,1024]{2,1,0:T(8,128)S(1)}, f32[16,8,1024]{2,1,0:T(8,128)}, u32[]{:S(2)}) copy-start(f32[16,8,1024]{2,1,0:T(8,128)} %tile.63) | copy-start | bytes 1572868
  154.1 21.7 %copy-start.11 = (f32[16,8,1024]{2,1,0:T(8,128)S(1)}, f32[16,8,1024]{2,1,0:T(8,128)}, u32[]{:S(2)}) copy-start(f32[16,8,1024]{2,1,0:T(8,128)} %tile.67) | copy-start | bytes 1572868
  154.6 21.2 %copy-start = (f32[16,8,1024]{2,1,0:T(8,128)}, f32[16,8,1024]{2,1,0:T(8,128)S(1)}, u32[]{:S(2)}) copy-start(f32[16,8,1024]{2,1,0:T(8,128)S(1)} %multiply_add_fusion.4) | copy-start | bytes 1572868
  154.7 4.8 collective-permute-start.6
  157.5 5.2 collective-permute-start.7
  162.8 6.8 collective-permute-start.8
  167.5 8.4 %collective-permute-start.9 = (f32[18,1,1024]{2,1,0:T(1,128)S(1)}, f32[18,1,1024]{2,1,0:T(1,128)S(1)}, u32[]{:S(2)}, u32[]{:S(2)}) collective-permute-start(f32[18,1,1024]{2,1,0:T(1,128)S(1)} %get-tuple-element.13), channel_id=1, source_target_pairs={{0,1},{1,2},{2,3},{3,4},{4,5},{5,6},{6,7},{7,8},{8,9},{9,10},{10,1... | collective-permute-start | bytes 221192 | tf_op jit(solution)/shard_map/ppermute | solution.py:23
  413.5 2.8 copy-start.6
  421.0 0.8 copy-start.1
  421.8 19.5 %copy-start.2 = (f32[16,8,1024]{2,1,0:T(8,128)S(1)}, f32[16,8,1024]{2,1,0:T(8,128)}, u32[]{:S(2)}) copy-start(f32[16,8,1024]{2,1,0:T(8,128)} %copy-done.1) | copy-start | bytes 1572868
  421.8 11.5 %collective-permute-start.10 = (f32[1,8,1024]{2,1,0:T(8,128)S(1)}, f32[1,8,1024]{2,1,0:T(8,128)S(1)}, u32[]{:S(2)}, u32[]{:S(2)}) collective-permute-start(f32[1,8,1024]{2,1,0:T(8,128)S(1)} %get-tuple-element.23), channel_id=1, source_target_pairs={{16,0},{32,16},{48,32},{64,48},{80,64},{96,80},{112,96},{128,112},... | collective-permute-start | bytes 98312 | tf_op jit(solution)/shard_map/ppermute | solution.py:26
  426.6 6.8 collective-permute-start.11
  434.8 11.6 %collective-permute-start.12 = (f32[18,1,1024]{2,1,0:T(1,128)S(1)}, f32[18,1,1024]{2,1,0:T(1,128)S(1)}, u32[]{:S(2)}, u32[]{:S(2)}) collective-permute-start(f32[18,1,1024]{2,1,0:T(1,128)S(1)} %get-tuple-element.10), channel_id=1, source_target_pairs={{1,0},{2,1},{3,2},{4,3},{5,4},{6,5},{7,6},{8,7},{9,8},{10,9},{11,1... | collective-permute-start | bytes 221192 | tf_op jit(solution)/shard_map/ppermute | solution.py:26
  439.4 8.4 %collective-permute-start.13 = (f32[18,1,1024]{2,1,0:T(1,128)S(1)}, f32[18,1,1024]{2,1,0:T(1,128)S(1)}, u32[]{:S(2)}, u32[]{:S(2)}) collective-permute-start(f32[18,1,1024]{2,1,0:T(1,128)S(1)} %get-tuple-element.11), channel_id=1, source_target_pairs={{0,1},{1,2},{2,3},{3,4},{4,5},{5,6},{6,7},{7,8},{8,9},{9,10},{10,1... | collective-permute-start | bytes 221192 | tf_op jit(solution)/shard_map/ppermute | solution.py:23
  450.7 6.9 copy-start.12
  459.4 145.1 %copy-start.4 = (f32[128,16,64]{0,1,2:T(8,128)S(1)}, f32[128,16,64]{0,1,2:T(8,128)}, u32[]{:S(2)}) copy-start(f32[128,16,64]{0,1,2:T(8,128)} %copy-done.3) | copy-start | bytes 1572868
  704.5 14.6 %copy-start.8 = (f32[16,8,1024]{2,1,0:T(8,128)S(1)}, f32[16,8,1024]{2,1,0:T(8,128)}, u32[]{:S(2)}) copy-start(f32[16,8,1024]{2,1,0:T(8,128)} %param.10) | copy-start | bytes 1572868
  720.4 25.3 %copy-start.9 = (f32[16,8,1024]{2,1,0:T(8,128)}, f32[16,8,1024]{2,1,0:T(8,128)S(1)}, u32[]{:S(2)}) copy-start(f32[16,8,1024]{2,1,0:T(8,128)S(1)} %add_add_fusion) | copy-start | bytes 1572868
  720.4 6.1 collective-permute-start.14
  724.5 5.2 collective-permute-start.15
  729.9 6.8 collective-permute-start.16
  734.5 8.4 %collective-permute-start.17 = (f32[18,1,1024]{2,1,0:T(1,128)S(1)}, f32[18,1,1024]{2,1,0:T(1,128)S(1)}, u32[]{:S(2)}, u32[]{:S(2)}) collective-permute-start(f32[18,1,1024]{2,1,0:T(1,128)S(1)} %get-tuple-element.9), channel_id=1, source_target_pairs={{0,1},{1,2},{2,3},{3,4},{4,5},{5,6},{6,7},{7,8},{8,9},{9,10},{10,1... | collective-permute-start | bytes 221192 | tf_op jit(solution)/shard_map/ppermute | solution.py:23
